TPU v7x, 512 devices: a whole 4x8x8 slice. The times are simulated.
512 devices in a mesh: section: 16 (over x_hi, y), dp: 8 (over z), mp: 4 (over x_lo, core).
Axes of the slice: x: 4 (x_hi: 2, x_lo: 2; x = x_hi * 2 + x_lo), y: 8, z: 8, core: 2. Of those that a mesh axis runs over, the one named last changes fastest.
Arguments:
- cotangent: bfloat16 [1024, 4096], P('dp', 'mp'), may hold values from -6 to 6
- saved_inputs: bfloat16 [16, 1024, 4096], P('section', 'dp', 'mp'), may hold values from -6 to 6
- pre_acts: bfloat16 [16, 1024, 4096], P('section', 'dp', 'mp'), may hold values from -8 to 8
- weights: bfloat16 [16, 4096, 4096], P('section', 'mp', 'dp'), may hold values from -0.046875 to 0.046875
- proj_in: bfloat16 [16, 4096, 64], P('section', 'mp'), may hold values from -0.09375 to 0.09375
- proj_out: bfloat16 [16, 4096, 64], P('section', 'mp'), may hold values from -0.09375 to 0.09375
- query_panels: float32 [16, 16, 4096], P('section', 'dp', 'mp'), may hold values from -4 to 4
- partners: int32 [8, 8], replicated, may hold values from 0 to 7, as said below
Outputs:
- train_panels: float32 [16, 32, 4096], P('section', 'dp', 'mp')
- scores: float32 [16, 8, 4], replicated
Inputs may be any that keep to these rules, and one draw needn't show every extreme that they name: The plan has 8 rounds: one round pairs every dp index with itself, and the others are the rounds of one round-robin plan of the 8 indices. The rows of partners hold each of these rounds once, in some order, so partners[r, partners[r, i]] = i.
All inputs are finite; a program needn't handle non-finite values.
Results may differ from a plain program's by a relative error of at most 0.02.
Values may be sent and summed in bfloat16 or wider, within the bound.
No kernel may reach another device: no remote copies, remote signals or barrier semaphores. Data moves between devices by JAX's collectives and lax.ppermute only.
A program may use at most 64 MiB of HBM per device.

v0:
```python
import math
import jax
import jax.numpy as jnp
from jax import lax
from jax.sharding import PartitionSpec as P

LEN = 32


def from_behind(block, axis, distance):
    devices = range(lax.axis_size(axis))
    route = [(i - distance, i) for i in devices if i - distance in devices]
    return lax.ppermute(block, axis, route)


def silu_slope(pre_state):
    sigma = jax.nn.sigmoid(pre_state)
    return sigma * (1.0 + pre_state * (1.0 - sigma))


def score_pair(query_rows, train_rows):
    return jnp.dot(query_rows, train_rows.T, precision=lax.Precision.HIGHEST)


def place_block(score_table, block, row_at, col_at):
    return lax.dynamic_update_slice(
        score_table,
        block[None, None],
        (jnp.asarray(row_at, jnp.int32), jnp.int32(col_at), jnp.int32(0), jnp.int32(0)),
    )


def body(cotangent, saved_inputs, pre_acts, weights, proj_in, proj_out, query_panels, partners):
    section_count = lax.axis_size("section")
    model_count = lax.axis_size("mp")
    data_count = lax.axis_size("dp")
    section_index = lax.axis_index("section")
    model_index = lax.axis_index("mp")
    data_index = lax.axis_index("dp")
    inputs = saved_inputs[0]
    pre_state = pre_acts[0]
    columns = inputs.shape[1]
    length = LEN
    examples = inputs.shape[0] // length
    low_rank = proj_in.shape[2]
    w_rows = lax.all_gather(weights[0], "dp", axis=1, tiled=True)
    step_count = examples + section_count - 1
    top_section = section_count - 1

    def advance(turn, carry):
        outgoing, stored, side_store = carry
        received = from_behind(outgoing, "section", -1)
        example_at = turn - (top_section - section_index)
        active = jnp.logical_and(example_at >= 0, example_at < examples)
        row_start = jnp.clip(example_at, 0, examples - 1) * length
        top_grad = lax.dynamic_slice_in_dim(cotangent, row_start, length, 0)
        delta_piece = jnp.where(section_index == top_section, top_grad, received)
        slopes = silu_slope(
            lax.dynamic_slice_in_dim(pre_state, row_start, length, 0).astype(jnp.float32)
        )
        grad_piece = (delta_piece.astype(jnp.float32) * slopes).astype(jnp.bfloat16)
        grad_full = lax.all_gather(grad_piece, "mp", axis=1, tiled=True)

        def through():
            back_term = lax.dot_general(
                grad_full, w_rows, (((1,), (1,)), ((), ())), preferred_element_type=jnp.float32
            )
            return (delta_piece.astype(jnp.float32) + back_term).astype(jnp.bfloat16)

        def skipped():
            return jnp.zeros_like(delta_piece)

        passed = lax.cond(active, through, skipped)
        previous = lax.dynamic_slice_in_dim(stored, row_start, length, 0)
        stored = lax.dynamic_update_slice_in_dim(
            stored, jnp.where(active, grad_piece, previous), row_start, 0
        )
        return (passed, stored, side_store)

    initial = (
        jnp.zeros((length, columns), jnp.bfloat16),
        jnp.zeros((inputs.shape[0], columns), jnp.bfloat16),
        jnp.zeros((inputs.shape[0], low_rank), jnp.float32),
    )
    final_state = lax.fori_loop(0, step_count, advance, initial)
    stored = final_state[1]
    side_store = final_state[2]
    in_part = jnp.dot(inputs, proj_in[0], preferred_element_type=jnp.float32)
    out_part = jnp.dot(stored, proj_out[0], preferred_element_type=jnp.float32)
    in_side, out_side = (
        lax.psum(in_part.astype(jnp.bfloat16), "mp").astype(jnp.float32),
        lax.psum(out_part.astype(jnp.bfloat16), "mp").astype(jnp.float32),
    )
    piece_rank = low_rank // model_count
    in_rows = lax.dynamic_slice_in_dim(in_side, model_index * piece_rank, piece_rank, 1)
    panels_here = jnp.einsum(
        "etr,etc->erc",
        in_rows.reshape(examples, length, piece_rank),
        out_side.reshape(examples, length, low_rank),
        precision=lax.Precision.HIGHEST,
    ) / math.sqrt(length)
    panels_here = panels_here.reshape(examples, piece_rank * low_rank)
    queries = query_panels[0]
    asked = queries.shape[0]
    rounds = partners.shape[0]
    score_scale = 1.0 / (low_rank * math.sqrt(section_count))
    score_table = jnp.zeros((data_count, rounds, asked, examples), jnp.float32)
    everyone = lax.all_gather(panels_here, "dp", axis=0, tiled=True).reshape(
        data_count, examples, -1
    )
    for round_at in range(rounds):
        partner = partners[round_at, data_index]
        chosen = lax.dynamic_index_in_dim(everyone, partner, 0, keepdims=False)
        score_table = place_block(score_table, score_pair(queries, chosen), data_index, round_at)
    summed = lax.psum(score_table * score_scale, ("section", "dp", "mp"))
    scores = summed.transpose(0, 2, 1, 3).reshape(data_count * asked, rounds, examples)
    return (panels_here[None], scores)


def solution(mesh):
    placed = (
        P("dp", "mp"),
        P("section", "dp", "mp"),
        P("section", "dp", "mp"),
        P("section", "mp", "dp"),
        P("section", "mp", None),
        P("section", "mp", None),
        P("section", "dp", "mp"),
        P(),
    )
    return jax.shard_map(
        body, mesh=mesh, in_specs=placed, out_specs=(P("section", "dp", "mp"), P()), check_vma=False
    )
```

profile of v0, /device:TPU:1, one launch (start us, length us, event | category | flops | bytes accessed | tf_op | source)
XLA Modules:
  0.0 635.7 jit_solution(11931362347134518088)
XLA Ops:
  7.9 1.7 constant_dynamic-slice_fusion.2
  25.3 87.9 %all-gather.4.cloned.1.call-done = bf16[1,1024,4096]{2,1,0:T(8,128)(2,1)} async-done(((bf16[1,1024,512]{2,1,0:T(8,128)(2,1)}), bf16[1,1024,4096]{2,1,0:T(8,128)(2,1)}) %all-gather.4.cloned.1.call-update) | async-done | bytes 8388624 | tf_op jit(solution)/shard_map/all_gather | solution.py:46
  113.8 380.4 %while.17 = (s32[]{:T(128)}, bf16[32,1024]{1,0:T(8,128)(2,1)}, bf16[128,1024]{1,0:T(8,128)(2,1)S(1)}, s32[]{:T(128)}, pred[]{:T(512)}, /*index=5*/bf16[128,1024]...) while((s32[]{:T(128)}, bf16[32,1024]{1,0:T(8,128)(2,1)}, ...), condition=%wide.region_4.5_spmd, body=%wide.region_1.4_spmd.sunk | while | flops 268959744 | bytes 9830719 | solution.py:85
  113.9 1.4 collective-permute-start
  115.3 3.9 collective-permute-done
  120.2 7.4 %all_gather.18 = bf16[32,4096]{1,0:T(8,128)(2,1)S(1)} all-gather(bf16[32,1024]{1,0:T(8,128)(2,1)S(1)} %get-tuple-element.282), channel_id=1, replica_groups=mesh['section'=16,'dp'=8,'mp'=4] {'mp'}, dimensions={1}, use_global_device_ids=true | all-gather | bytes 327680 | tf_op jit(solution)/shard_map/while/body/eval_jaxpr/all_gather | solution.py:62
  128.2 1.3 collective-permute-start
  129.6 4.3 collective-permute-done
  134.8 6.6 %all_gather.18 = bf16[32,4096]{1,0:T(8,128)(2,1)S(1)} all-gather(bf16[32,1024]{1,0:T(8,128)(2,1)S(1)} %get-tuple-element.282), channel_id=1, replica_groups=mesh['section'=16,'dp'=8,'mp'=4] {'mp'}, dimensions={1}, use_global_device_ids=true | all-gather | bytes 327680 | tf_op jit(solution)/shard_map/while/body/eval_jaxpr/all_gather | solution.py:62
  142.1 1.3 collective-permute-start
  143.4 4.3 collective-permute-done
  148.7 6.6 %all_gather.18 = bf16[32,4096]{1,0:T(8,128)(2,1)S(1)} all-gather(bf16[32,1024]{1,0:T(8,128)(2,1)S(1)} %get-tuple-element.282), channel_id=1, replica_groups=mesh['section'=16,'dp'=8,'mp'=4] {'mp'}, dimensions={1}, use_global_device_ids=true | all-gather | bytes 327680 | tf_op jit(solution)/shard_map/while/body/eval_jaxpr/all_gather | solution.py:62
  155.9 1.3 collective-permute-start
  157.2 5.0 collective-permute-done
  163.2 6.4 %all_gather.18 = bf16[32,4096]{1,0:T(8,128)(2,1)S(1)} all-gather(bf16[32,1024]{1,0:T(8,128)(2,1)S(1)} %get-tuple-element.282), channel_id=1, replica_groups=mesh['section'=16,'dp'=8,'mp'=4] {'mp'}, dimensions={1}, use_global_device_ids=true | all-gather | bytes 327680 | tf_op jit(solution)/shard_map/while/body/eval_jaxpr/all_gather | solution.py:62
  170.1 1.3 collective-permute-start
  171.5 5.8 collective-permute-done
  178.2 6.4 %all_gather.18 = bf16[32,4096]{1,0:T(8,128)(2,1)S(1)} all-gather(bf16[32,1024]{1,0:T(8,128)(2,1)S(1)} %get-tuple-element.282), channel_id=1, replica_groups=mesh['section'=16,'dp'=8,'mp'=4] {'mp'}, dimensions={1}, use_global_device_ids=true | all-gather | bytes 327680 | tf_op jit(solution)/shard_map/while/body/eval_jaxpr/all_gather | solution.py:62
  185.2 1.3 collective-permute-start
  186.5 5.8 collective-permute-done
  193.2 6.4 %all_gather.18 = bf16[32,4096]{1,0:T(8,128)(2,1)S(1)} all-gather(bf16[32,1024]{1,0:T(8,128)(2,1)S(1)} %get-tuple-element.282), channel_id=1, replica_groups=mesh['section'=16,'dp'=8,'mp'=4] {'mp'}, dimensions={1}, use_global_device_ids=true | all-gather | bytes 327680 | tf_op jit(solution)/shard_map/while/body/eval_jaxpr/all_gather | solution.py:62
  200.2 1.3 collective-permute-start
  201.5 5.8 collective-permute-done
  208.2 6.4 %all_gather.18 = bf16[32,4096]{1,0:T(8,128)(2,1)S(1)} all-gather(bf16[32,1024]{1,0:T(8,128)(2,1)S(1)} %get-tuple-element.282), channel_id=1, replica_groups=mesh['section'=16,'dp'=8,'mp'=4] {'mp'}, dimensions={1}, use_global_device_ids=true | all-gather | bytes 327680 | tf_op jit(solution)/shard_map/while/body/eval_jaxpr/all_gather | solution.py:62
  215.2 1.3 collective-permute-start
  216.5 5.8 collective-permute-done
  223.2 6.4 %all_gather.18 = bf16[32,4096]{1,0:T(8,128)(2,1)S(1)} all-gather(bf16[32,1024]{1,0:T(8,128)(2,1)S(1)} %get-tuple-element.282), channel_id=1, replica_groups=mesh['section'=16,'dp'=8,'mp'=4] {'mp'}, dimensions={1}, use_global_device_ids=true | all-gather | bytes 327680 | tf_op jit(solution)/shard_map/while/body/eval_jaxpr/all_gather | solution.py:62
  230.2 1.3 collective-permute-start
  231.5 5.8 collective-permute-done
  238.3 6.4 %all_gather.18 = bf16[32,4096]{1,0:T(8,128)(2,1)S(1)} all-gather(bf16[32,1024]{1,0:T(8,128)(2,1)S(1)} %get-tuple-element.282), channel_id=1, replica_groups=mesh['section'=16,'dp'=8,'mp'=4] {'mp'}, dimensions={1}, use_global_device_ids=true | all-gather | bytes 327680 | tf_op jit(solution)/shard_map/while/body/eval_jaxpr/all_gather | solution.py:62
  245.3 1.3 collective-permute-start
  246.6 5.8 collective-permute-done
  253.3 6.4 %all_gather.18 = bf16[32,4096]{1,0:T(8,128)(2,1)S(1)} all-gather(bf16[32,1024]{1,0:T(8,128)(2,1)S(1)} %get-tuple-element.282), channel_id=1, replica_groups=mesh['section'=16,'dp'=8,'mp'=4] {'mp'}, dimensions={1}, use_global_device_ids=true | all-gather | bytes 327680 | tf_op jit(solution)/shard_map/while/body/eval_jaxpr/all_gather | solution.py:62
  260.3 1.3 collective-permute-start
  261.6 8.1 %collective-permute-done = bf16[32,1024]{1,0:T(8,128)(2,1)S(1)} collective-permute-done((bf16[32,1024]{1,0:T(8,128)(2,1)}, bf16[32,1024]{1,0:T(8,128)(2,1)S(1)}, u32[]{:S(2)}, u32[]{:S(2)}) %collective-permute-start) | collective-permute-done | bytes 65568 | tf_op jit(solution)/shard_map/while/body/eval_jaxpr/ppermute | solution.py:13
  270.6 6.4 %all_gather.18 = bf16[32,4096]{1,0:T(8,128)(2,1)S(1)} all-gather(bf16[32,1024]{1,0:T(8,128)(2,1)S(1)} %get-tuple-element.282), channel_id=1, replica_groups=mesh['section'=16,'dp'=8,'mp'=4] {'mp'}, dimensions={1}, use_global_device_ids=true | all-gather | bytes 327680 | tf_op jit(solution)/shard_map/while/body/eval_jaxpr/all_gather | solution.py:62
  277.6 1.3 collective-permute-start
  278.9 8.2 %collective-permute-done = bf16[32,1024]{1,0:T(8,128)(2,1)S(1)} collective-permute-done((bf16[32,1024]{1,0:T(8,128)(2,1)}, bf16[32,1024]{1,0:T(8,128)(2,1)S(1)}, u32[]{:S(2)}, u32[]{:S(2)}) %collective-permute-start) | collective-permute-done | bytes 65568 | tf_op jit(solution)/shard_map/while/body/eval_jaxpr/ppermute | solution.py:13
  288.0 6.4 %all_gather.18 = bf16[32,4096]{1,0:T(8,128)(2,1)S(1)} all-gather(bf16[32,1024]{1,0:T(8,128)(2,1)S(1)} %get-tuple-element.282), channel_id=1, replica_groups=mesh['section'=16,'dp'=8,'mp'=4] {'mp'}, dimensions={1}, use_global_device_ids=true | all-gather | bytes 327680 | tf_op jit(solution)/shard_map/while/body/eval_jaxpr/all_gather | solution.py:62
  296.3 8.2 %collective-permute-done = bf16[32,1024]{1,0:T(8,128)(2,1)S(1)} collective-permute-done((bf16[32,1024]{1,0:T(8,128)(2,1)}, bf16[32,1024]{1,0:T(8,128)(2,1)S(1)}, u32[]{:S(2)}, u32[]{:S(2)}) %collective-permute-start) | collective-permute-done | bytes 65568 | tf_op jit(solution)/shard_map/while/body/eval_jaxpr/ppermute | solution.py:13
  305.5 6.4 %all_gather.18 = bf16[32,4096]{1,0:T(8,128)(2,1)S(1)} all-gather(bf16[32,1024]{1,0:T(8,128)(2,1)S(1)} %get-tuple-element.282), channel_id=1, replica_groups=mesh['section'=16,'dp'=8,'mp'=4] {'mp'}, dimensions={1}, use_global_device_ids=true | all-gather | bytes 327680 | tf_op jit(solution)/shard_map/while/body/eval_jaxpr/all_gather | solution.py:62
  313.8 8.2 %collective-permute-done = bf16[32,1024]{1,0:T(8,128)(2,1)S(1)} collective-permute-done((bf16[32,1024]{1,0:T(8,128)(2,1)}, bf16[32,1024]{1,0:T(8,128)(2,1)S(1)}, u32[]{:S(2)}, u32[]{:S(2)}) %collective-permute-start) | collective-permute-done | bytes 65568 | tf_op jit(solution)/shard_map/while/body/eval_jaxpr/ppermute | solution.py:13
  322.9 6.4 %all_gather.18 = bf16[32,4096]{1,0:T(8,128)(2,1)S(1)} all-gather(bf16[32,1024]{1,0:T(8,128)(2,1)S(1)} %get-tuple-element.282), channel_id=1, replica_groups=mesh['section'=16,'dp'=8,'mp'=4] {'mp'}, dimensions={1}, use_global_device_ids=true | all-gather | bytes 327680 | tf_op jit(solution)/shard_map/while/body/eval_jaxpr/all_gather | solution.py:62
  331.2 8.2 %collective-permute-done = bf16[32,1024]{1,0:T(8,128)(2,1)S(1)} collective-permute-done((bf16[32,1024]{1,0:T(8,128)(2,1)}, bf16[32,1024]{1,0:T(8,128)(2,1)S(1)}, u32[]{:S(2)}, u32[]{:S(2)}) %collective-permute-start) | collective-permute-done | bytes 65568 | tf_op jit(solution)/shard_map/while/body/eval_jaxpr/ppermute | solution.py:13
  340.3 6.4 %all_gather.18 = bf16[32,4096]{1,0:T(8,128)(2,1)S(1)} all-gather(bf16[32,1024]{1,0:T(8,128)(2,1)S(1)} %get-tuple-element.282), channel_id=1, replica_groups=mesh['section'=16,'dp'=8,'mp'=4] {'mp'}, dimensions={1}, use_global_device_ids=true | all-gather | bytes 327680 | tf_op jit(solution)/shard_map/while/body/eval_jaxpr/all_gather | solution.py:62
  348.6 61.6 %collective-permute-done = bf16[32,1024]{1,0:T(8,128)(2,1)S(1)} collective-permute-done((bf16[32,1024]{1,0:T(8,128)(2,1)}, bf16[32,1024]{1,0:T(8,128)(2,1)S(1)}, u32[]{:S(2)}, u32[]{:S(2)}) %collective-permute-start) | collective-permute-done | bytes 65568 | tf_op jit(solution)/shard_map/while/body/eval_jaxpr/ppermute | solution.py:13
  411.2 6.3 all_gather.18
  417.5 6.6 %conditional.2 = (bf16[32,1024]{1,0:T(8,128)(2,1)}) conditional(s32[]{:T(128)} %convert_element_type.80, () %tuple.60, (bf16[32,1024]{1,0:T(8,128)(2,1)S(1)}, bf16[32,4096]{1,0:T(8,128)(2,1)S(1)}, bf16[1024,4096]{1,0:T(8,128)(2,1)}) %tuple.61), branch_computations={%region_2.2_spmd, %region_3.3_spmd} | conditional | flops 268533760 | bytes 8781832 | solution.py:73
  417.5 6.6 %fusion = bf16[32,1024]{1,0:T(8,128)(2,1)} fusion(bf16[32,4096]{1,0:T(8,128)(2,1)S(1)} %get-tuple-element.181, bf16[1024,4096]{1,0:T(8,128)(2,1)} %get-tuple-element.182, bf16[32,1024]{1,0:T(8,128)(2,1)S(1)} %get-tuple-element.180), kind=kOutput, calls=%fused_computation.1 | convolution fusion | flops 268533760 | bytes 8781824 | tf_op jit(solution)/shard_map/while/body/eval_jaxpr/cond/branch_1_fun/dot_general | solution.py:65
  425.4 8.2 %collective-permute-done = bf16[32,1024]{1,0:T(8,128)(2,1)S(1)} collective-permute-done((bf16[32,1024]{1,0:T(8,128)(2,1)}, bf16[32,1024]{1,0:T(8,128)(2,1)S(1)}, u32[]{:S(2)}, u32[]{:S(2)}) %collective-permute-start) | collective-permute-done | bytes 65568 | tf_op jit(solution)/shard_map/while/body/eval_jaxpr/ppermute | solution.py:13
  434.6 6.3 all_gather.18
  440.8 6.6 %conditional.2 = (bf16[32,1024]{1,0:T(8,128)(2,1)}) conditional(s32[]{:T(128)} %convert_element_type.80, () %tuple.60, (bf16[32,1024]{1,0:T(8,128)(2,1)S(1)}, bf16[32,4096]{1,0:T(8,128)(2,1)S(1)}, bf16[1024,4096]{1,0:T(8,128)(2,1)}) %tuple.61), branch_computations={%region_2.2_spmd, %region_3.3_spmd} | conditional | flops 268533760 | bytes 8781832 | solution.py:73
  440.8 6.6 %fusion = bf16[32,1024]{1,0:T(8,128)(2,1)} fusion(bf16[32,4096]{1,0:T(8,128)(2,1)S(1)} %get-tuple-element.181, bf16[1024,4096]{1,0:T(8,128)(2,1)} %get-tuple-element.182, bf16[32,1024]{1,0:T(8,128)(2,1)S(1)} %get-tuple-element.180), kind=kOutput, calls=%fused_computation.1 | convolution fusion | flops 268533760 | bytes 8781824 | tf_op jit(solution)/shard_map/while/body/eval_jaxpr/cond/branch_1_fun/dot_general | solution.py:65
  448.7 8.3 %collective-permute-done = bf16[32,1024]{1,0:T(8,128)(2,1)S(1)} collective-permute-done((bf16[32,1024]{1,0:T(8,128)(2,1)}, bf16[32,1024]{1,0:T(8,128)(2,1)S(1)}, u32[]{:S(2)}, u32[]{:S(2)}) %collective-permute-start) | collective-permute-done | bytes 65568 | tf_op jit(solution)/shard_map/while/body/eval_jaxpr/ppermute | solution.py:13
  458.0 6.3 all_gather.18
  464.3 6.6 %conditional.2 = (bf16[32,1024]{1,0:T(8,128)(2,1)}) conditional(s32[]{:T(128)} %convert_element_type.80, () %tuple.60, (bf16[32,1024]{1,0:T(8,128)(2,1)S(1)}, bf16[32,4096]{1,0:T(8,128)(2,1)S(1)}, bf16[1024,4096]{1,0:T(8,128)(2,1)}) %tuple.61), branch_computations={%region_2.2_spmd, %region_3.3_spmd} | conditional | flops 268533760 | bytes 8781832 | solution.py:73
  464.3 6.6 %fusion = bf16[32,1024]{1,0:T(8,128)(2,1)} fusion(bf16[32,4096]{1,0:T(8,128)(2,1)S(1)} %get-tuple-element.181, bf16[1024,4096]{1,0:T(8,128)(2,1)} %get-tuple-element.182, bf16[32,1024]{1,0:T(8,128)(2,1)S(1)} %get-tuple-element.180), kind=kOutput, calls=%fused_computation.1 | convolution fusion | flops 268533760 | bytes 8781824 | tf_op jit(solution)/shard_map/while/body/eval_jaxpr/cond/branch_1_fun/dot_general | solution.py:65
  472.2 8.2 %collective-permute-done = bf16[32,1024]{1,0:T(8,128)(2,1)S(1)} collective-permute-done((bf16[32,1024]{1,0:T(8,128)(2,1)}, bf16[32,1024]{1,0:T(8,128)(2,1)S(1)}, u32[]{:S(2)}, u32[]{:S(2)}) %collective-permute-start) | collective-permute-done | bytes 65568 | tf_op jit(solution)/shard_map/while/body/eval_jaxpr/ppermute | solution.py:13
  481.4 6.3 all_gather.18
  487.7 6.6 %conditional.2 = (bf16[32,1024]{1,0:T(8,128)(2,1)}) conditional(s32[]{:T(128)} %convert_element_type.80, () %tuple.60, (bf16[32,1024]{1,0:T(8,128)(2,1)S(1)}, bf16[32,4096]{1,0:T(8,128)(2,1)S(1)}, bf16[1024,4096]{1,0:T(8,128)(2,1)}) %tuple.61), branch_computations={%region_2.2_spmd, %region_3.3_spmd} | conditional | flops 268533760 | bytes 8781832 | solution.py:73
  487.7 6.6 %fusion = bf16[32,1024]{1,0:T(8,128)(2,1)} fusion(bf16[32,4096]{1,0:T(8,128)(2,1)S(1)} %get-tuple-element.181, bf16[1024,4096]{1,0:T(8,128)(2,1)} %get-tuple-element.182, bf16[32,1024]{1,0:T(8,128)(2,1)S(1)} %get-tuple-element.180), kind=kOutput, calls=%fused_computation.1 | convolution fusion | flops 268533760 | bytes 8781824 | tf_op jit(solution)/shard_map/while/body/eval_jaxpr/cond/branch_1_fun/dot_general | solution.py:65
  494.6 10.8 %all-reduce = (bf16[4,32,64]{2,1,0:T(8,128)(2,1)S(1)}, bf16[128,64]{0,1:T(8,128)(2,1)S(1)}) all-reduce(bf16[4,32,64]{2,1,0:T(8,128)(2,1)S(1)} %bitcast.104, bf16[128,64]{0,1:T(8,128)(2,1)S(1)} %convolution_convert_fusion.1), channel_id=1, replica_groups=mesh['section'=16,'dp'=8,'mp'=4] {'mp'}, use_global_device_ids=true, to_apply=%region_5.6 | all-reduce | flops 16384 | bytes 65536 | tf_op jit(solution)/shard_map/psum | solution.py:92
  505.7 18.5 %all-gather.1 = f32[8,4,1024]{2,1,0:T(4,128)S(1)} all-gather(f32[1,4,1024]{2,1,0:T(4,128)S(1)} %broadcast_in_dim_reshape.3), channel_id=1, replica_groups=mesh['section'=16,'dp'=8,'mp'=4] {'dp'}, dimensions={0}, use_global_device_ids=true | all-gather | bytes 147456 | tf_op jit(solution)/shard_map/all_gather | solution.py:108
  529.0 99.2 %psum.23 = f32[16,8,4]{1,0,2:T(8,128)S(1)} all-reduce(f32[16,8,4]{1,0,2:T(8,128)S(1)} %bitcast.105), channel_id=1, replica_groups=mesh['section'=16,'dp'=8,'mp'=4] {'section','dp','mp'}, use_global_device_ids=true, to_apply=%region_6.7 | all-reduce | flops 512 | bytes 4096 | tf_op jit(solution)/shard_map/psum | solution.py:115
  (102 shorter events, 54.5 us)
Async XLA Ops:
  7.2 17.0 %copy-start = (bf16[1,128,1024]{2,1,0:T(8,128)(2,1)S(1)}, bf16[1,128,1024]{2,1,0:T(8,128)(2,1)}, u32[]{:S(2)}) copy-start(bf16[1,128,1024]{2,1,0:T(8,128)(2,1)} %param.13) | copy-start | bytes 786436
  7.2 106.0 %all-gather.4.cloned.1.call-start = ((), (), s32[]{:S(2)}) async-start(), calls=%async_computation | async-start | bytes 9437184 | tf_op jit(solution)/shard_map/all_gather | solution.py:46
  113.8 380.5 %copy-start.2 = (bf16[1,1024,64]{1,2,0:T(8,128)(2,1)S(1)}, bf16[1,1024,64]{1,2,0:T(8,128)(2,1)}, u32[]{:S(2)}) copy-start(bf16[1,1024,64]{1,2,0:T(8,128)(2,1)} %param.17) | copy-start | bytes 393220
  113.8 410.4 %copy-start.1 = (f32[1,2,1024]{2,1,0:T(2,128)S(1)}, f32[1,2,1024]{2,1,0:T(2,128)}, u32[]{:S(2)}) copy-start(f32[1,2,1024]{2,1,0:T(2,128)} %param.18) | copy-start | bytes 24580
  113.9 5.4 collective-permute-start
  128.2 5.6 collective-permute-start
  142.1 5.6 collective-permute-start
  155.9 6.3 collective-permute-start
  170.1 7.1 %collective-permute-start = (bf16[32,1024]{1,0:T(8,128)(2,1)}, bf16[32,1024]{1,0:T(8,128)(2,1)S(1)}, u32[]{:S(2)}, u32[]{:S(2)}) collective-permute-start(bf16[32,1024]{1,0:T(8,128)(2,1)} %get-tuple-element.299), channel_id=1, source_target_pairs={{32,0},{64,32},{96,64},{128,96},{160,128},{192,160},{224,192},{256... | collective-permute-start | bytes 196616 | tf_op jit(solution)/shard_map/while/body/eval_jaxpr/ppermute | solution.py:13
  185.2 7.1 %collective-permute-start = (bf16[32,1024]{1,0:T(8,128)(2,1)}, bf16[32,1024]{1,0:T(8,128)(2,1)S(1)}, u32[]{:S(2)}, u32[]{:S(2)}) collective-permute-start(bf16[32,1024]{1,0:T(8,128)(2,1)} %get-tuple-element.299), channel_id=1, source_target_pairs={{32,0},{64,32},{96,64},{128,96},{160,128},{192,160},{224,192},{256... | collective-permute-start | bytes 196616 | tf_op jit(solution)/shard_map/while/body/eval_jaxpr/ppermute | solution.py:13
  200.2 7.1 %collective-permute-start = (bf16[32,1024]{1,0:T(8,128)(2,1)}, bf16[32,1024]{1,0:T(8,128)(2,1)S(1)}, u32[]{:S(2)}, u32[]{:S(2)}) collective-permute-start(bf16[32,1024]{1,0:T(8,128)(2,1)} %get-tuple-element.299), channel_id=1, source_target_pairs={{32,0},{64,32},{96,64},{128,96},{160,128},{192,160},{224,192},{256... | collective-permute-start | bytes 196616 | tf_op jit(solution)/shard_map/while/body/eval_jaxpr/ppermute | solution.py:13
  215.2 7.1 %collective-permute-start = (bf16[32,1024]{1,0:T(8,128)(2,1)}, bf16[32,1024]{1,0:T(8,128)(2,1)S(1)}, u32[]{:S(2)}, u32[]{:S(2)}) collective-permute-start(bf16[32,1024]{1,0:T(8,128)(2,1)} %get-tuple-element.299), channel_id=1, source_target_pairs={{32,0},{64,32},{96,64},{128,96},{160,128},{192,160},{224,192},{256... | collective-permute-start | bytes 196616 | tf_op jit(solution)/shard_map/while/body/eval_jaxpr/ppermute | solution.py:13
  230.2 7.1 %collective-permute-start = (bf16[32,1024]{1,0:T(8,128)(2,1)}, bf16[32,1024]{1,0:T(8,128)(2,1)S(1)}, u32[]{:S(2)}, u32[]{:S(2)}) collective-permute-start(bf16[32,1024]{1,0:T(8,128)(2,1)} %get-tuple-element.299), channel_id=1, source_target_pairs={{32,0},{64,32},{96,64},{128,96},{160,128},{192,160},{224,192},{256... | collective-permute-start | bytes 196616 | tf_op jit(solution)/shard_map/while/body/eval_jaxpr/ppermute | solution.py:13
  245.3 7.1 %collective-permute-start = (bf16[32,1024]{1,0:T(8,128)(2,1)}, bf16[32,1024]{1,0:T(8,128)(2,1)S(1)}, u32[]{:S(2)}, u32[]{:S(2)}) collective-permute-start(bf16[32,1024]{1,0:T(8,128)(2,1)} %get-tuple-element.299), channel_id=1, source_target_pairs={{32,0},{64,32},{96,64},{128,96},{160,128},{192,160},{224,192},{256... | collective-permute-start | bytes 196616 | tf_op jit(solution)/shard_map/while/body/eval_jaxpr/ppermute | solution.py:13
  260.3 9.4 %collective-permute-start = (bf16[32,1024]{1,0:T(8,128)(2,1)}, bf16[32,1024]{1,0:T(8,128)(2,1)S(1)}, u32[]{:S(2)}, u32[]{:S(2)}) collective-permute-start(bf16[32,1024]{1,0:T(8,128)(2,1)} %get-tuple-element.299), channel_id=1, source_target_pairs={{32,0},{64,32},{96,64},{128,96},{160,128},{192,160},{224,192},{256... | collective-permute-start | bytes 196616 | tf_op jit(solution)/shard_map/while/body/eval_jaxpr/ppermute | solution.py:13
  277.6 9.5 %collective-permute-start = (bf16[32,1024]{1,0:T(8,128)(2,1)}, bf16[32,1024]{1,0:T(8,128)(2,1)S(1)}, u32[]{:S(2)}, u32[]{:S(2)}) collective-permute-start(bf16[32,1024]{1,0:T(8,128)(2,1)} %get-tuple-element.299), channel_id=1, source_target_pairs={{32,0},{64,32},{96,64},{128,96},{160,128},{192,160},{224,192},{256... | collective-permute-start | bytes 196616 | tf_op jit(solution)/shard_map/while/body/eval_jaxpr/ppermute | solution.py:13
  295.0 9.5 %collective-permute-start = (bf16[32,1024]{1,0:T(8,128)(2,1)}, bf16[32,1024]{1,0:T(8,128)(2,1)S(1)}, u32[]{:S(2)}, u32[]{:S(2)}) collective-permute-start(bf16[32,1024]{1,0:T(8,128)(2,1)} %get-tuple-element.299), channel_id=1, source_target_pairs={{32,0},{64,32},{96,64},{128,96},{160,128},{192,160},{224,192},{256... | collective-permute-start | bytes 196616 | tf_op jit(solution)/shard_map/while/body/eval_jaxpr/ppermute | solution.py:13
  312.4 9.5 %collective-permute-start = (bf16[32,1024]{1,0:T(8,128)(2,1)}, bf16[32,1024]{1,0:T(8,128)(2,1)S(1)}, u32[]{:S(2)}, u32[]{:S(2)}) collective-permute-start(bf16[32,1024]{1,0:T(8,128)(2,1)} %get-tuple-element.299), channel_id=1, source_target_pairs={{32,0},{64,32},{96,64},{128,96},{160,128},{192,160},{224,192},{256... | collective-permute-start | bytes 196616 | tf_op jit(solution)/shard_map/while/body/eval_jaxpr/ppermute | solution.py:13
  329.9 9.5 %collective-permute-start = (bf16[32,1024]{1,0:T(8,128)(2,1)}, bf16[32,1024]{1,0:T(8,128)(2,1)S(1)}, u32[]{:S(2)}, u32[]{:S(2)}) collective-permute-start(bf16[32,1024]{1,0:T(8,128)(2,1)} %get-tuple-element.299), channel_id=1, source_target_pairs={{32,0},{64,32},{96,64},{128,96},{160,128},{192,160},{224,192},{256... | collective-permute-start | bytes 196616 | tf_op jit(solution)/shard_map/while/body/eval_jaxpr/ppermute | solution.py:13
  347.3 62.9 %collective-permute-start = (bf16[32,1024]{1,0:T(8,128)(2,1)}, bf16[32,1024]{1,0:T(8,128)(2,1)S(1)}, u32[]{:S(2)}, u32[]{:S(2)}) collective-permute-start(bf16[32,1024]{1,0:T(8,128)(2,1)} %get-tuple-element.299), channel_id=1, source_target_pairs={{32,0},{64,32},{96,64},{128,96},{160,128},{192,160},{224,192},{256... | collective-permute-start | bytes 196616 | tf_op jit(solution)/shard_map/while/body/eval_jaxpr/ppermute | solution.py:13
  424.0 9.6 %collective-permute-start = (bf16[32,1024]{1,0:T(8,128)(2,1)}, bf16[32,1024]{1,0:T(8,128)(2,1)S(1)}, u32[]{:S(2)}, u32[]{:S(2)}) collective-permute-start(bf16[32,1024]{1,0:T(8,128)(2,1)} %get-tuple-element.299), channel_id=1, source_target_pairs={{32,0},{64,32},{96,64},{128,96},{160,128},{192,160},{224,192},{256... | collective-permute-start | bytes 196616 | tf_op jit(solution)/shard_map/while/body/eval_jaxpr/ppermute | solution.py:13
  447.4 9.6 %collective-permute-start = (bf16[32,1024]{1,0:T(8,128)(2,1)}, bf16[32,1024]{1,0:T(8,128)(2,1)S(1)}, u32[]{:S(2)}, u32[]{:S(2)}) collective-permute-start(bf16[32,1024]{1,0:T(8,128)(2,1)} %get-tuple-element.299), channel_id=1, source_target_pairs={{32,0},{64,32},{96,64},{128,96},{160,128},{192,160},{224,192},{256... | collective-permute-start | bytes 196616 | tf_op jit(solution)/shard_map/while/body/eval_jaxpr/ppermute | solution.py:13
  470.9 9.6 %collective-permute-start = (bf16[32,1024]{1,0:T(8,128)(2,1)}, bf16[32,1024]{1,0:T(8,128)(2,1)S(1)}, u32[]{:S(2)}, u32[]{:S(2)}) collective-permute-start(bf16[32,1024]{1,0:T(8,128)(2,1)} %get-tuple-element.299), channel_id=1, source_target_pairs={{32,0},{64,32},{96,64},{128,96},{160,128},{192,160},{224,192},{256... | collective-permute-start | bytes 196616 | tf_op jit(solution)/shard_map/while/body/eval_jaxpr/ppermute | solution.py:13
  505.7 123.2 %copy-start.3 = (f32[1,4,1024]{2,1,0:T(4,128)}, f32[1,4,1024]{2,1,0:T(4,128)S(1)}, u32[]{:S(2)}) copy-start(f32[1,4,1024]{2,1,0:T(4,128)S(1)} %broadcast_in_dim_reshape.3) | copy-start | bytes 49156
Sparse Core Ops, SparseCore 0:
  10.1 103.0 all-gather.3
where the time goes:
time: 638 us; the launch traced here: 636 us
  waiting for transfers between devices  268 us (42%)
  blocking collectives  251 us (39%)
  matrix products  29.3 us (5%)
  between operations  28.8 us (5%)
  starting transfers between devices  24.5 us (4%)
  other arithmetic  18.2 us (3%)
  local copies, waits for them, and re-layouts  15.9 us (2%)
    ppermute x19, waiting for transfers between devices, from_behind(): return lax.ppermute(block, axis, route)  179 us
    all_gather x19, blocking collectives, advance(): grad_full = lax.all_gather(grad_piece, 'mp', axis=1, tiled=True)  122 us
    psum x1, blocking collectives, body(): summed = lax.psum(score_table * score_scale, ('section', 'dp', 'mp'))  99.2 us
    all_gather x1, waiting for transfers between devices, body(): w_rows = lax.all_gather(weights[0], 'dp', axis=1, tiled=True)  87.9 us
    dot_general x4, matrix products, through(): lax.dot_general(grad_full, w_rows, (((1,), (1,)), ((), ())), preferred_el...  26.4 us
    ppermute x19, starting transfers between devices, from_behind(): return lax.ppermute(block, axis, route)  24.5 us
    all_gather x1, blocking collectives, body(): lax.all_gather(panels_here, 'dp', axis=0, tiled=True)  18.5 us
    dynamic_update_slice x19, other arithmetic, advance(): lax.dynamic_update_slice_in_dim(stored, jnp.where(active, grad_piece, pre...  18.2 us
  transfers between devices with their start and end apart: 20, of which 20 were waited for; matrix products, arithmetic and copies ran while one was open for 0% of the time, Pallas kernels for 0%

commit v1 on v0

--- a/solution.py
+++ b/solution.py
@@ -112,7 +112,7 @@
         partner = partners[round_at, data_index]
         chosen = lax.dynamic_index_in_dim(everyone, partner, 0, keepdims=False)
         score_table = place_block(score_table, score_pair(queries, chosen), data_index, round_at)
-    summed = lax.psum(score_table * score_scale, ("section", "dp", "mp"))
+    summed = jnp.sum(lax.all_gather(score_table * score_scale, ("section", "dp", "mp")), axis=0)
     scores = summed.transpose(0, 2, 1, 3).reshape(data_count * asked, rounds, examples)
     return (panels_here[None], scores)
 

time: 638 us -> 1380 us (2.16)
  waiting for transfers between devices: 268 us -> 1090 us
  blocking collectives: 251 us -> 152 us
    all_gather x0 -> x1, waiting for transfers between devices: none -> 824 us  [body(): lax.all_gather(score_table * score_scale, ('section', 'dp', 'mp'))]
    psum x1 -> x0, blocking collectives: 99.2 us -> none  [body(): summed = lax.psum(score_table * score_scale, ('section', 'dp', 'mp'))]
  transfers between devices with their start and end apart: 20 -> 21, of which waited for: 20 -> 21; matrix products, arithmetic and copies ran while one was open for 0% -> 0% of each run, Pallas kernels for 0% -> 0%
where the time goes in v1:
time: 1380 us; the launch traced here: 1370 us
  waiting for transfers between devices  1090 us (79%)
  blocking collectives  152 us (11%)
  matrix products  29.3 us (2%)
  other arithmetic  28.7 us (2%)
  between operations  28.6 us (2%)
  starting transfers between devices  24.5 us (2%)
  local copies, waits for them, and re-layouts  14.8 us (1%)
    all_gather x1, waiting for transfers between devices, body(): lax.all_gather(score_table * score_scale, ('section', 'dp', 'mp'))  824 us
    ppermute x19, waiting for transfers between devices, from_behind(): return lax.ppermute(block, axis, route)  179 us
    all_gather x19, blocking collectives, advance(): grad_full = lax.all_gather(grad_piece, 'mp', axis=1, tiled=True)  122 us
    all_gather x1, waiting for transfers between devices, body(): w_rows = lax.all_gather(weights[0], 'dp', axis=1, tiled=True)  88 us
  transfers between devices with their start and end apart: 21, of which 21 were waited for; matrix products, arithmetic and copies ran while one was open for 0% of the time, Pallas kernels for 0%

profile of v1, /device:TPU:1, one launch (start us, length us, event | category | flops | bytes accessed | tf_op | source)
XLA Modules:
  0.0 1369.8 jit_solution(1747370281964039505)
XLA Ops:
  8.0 1.6 constant_dynamic-slice_fusion.2
  25.2 88.0 %all-gather.6.cloned.1.call-done = bf16[1,1024,4096]{2,1,0:T(8,128)(2,1)} async-done(((bf16[1,1024,512]{2,1,0:T(8,128)(2,1)}), bf16[1,1024,4096]{2,1,0:T(8,128)(2,1)}) %all-gather.6.cloned.1.call-update) | async-done | bytes 8388624 | tf_op jit(solution)/shard_map/all_gather | solution.py:46
  113.8 380.4 %while.17 = (s32[]{:T(128)}, bf16[32,1024]{1,0:T(8,128)(2,1)}, bf16[128,1024]{1,0:T(8,128)(2,1)S(1)}, s32[]{:T(128)}, pred[]{:T(512)}, /*index=5*/bf16[128,1024]...) while((s32[]{:T(128)}, bf16[32,1024]{1,0:T(8,128)(2,1)}, ...), condition=%wide.region_4.5_spmd, body=%wide.region_1.4_spmd.sunk | while | flops 268959744 | bytes 9830719 | solution.py:85
  113.9 1.4 collective-permute-start
  115.3 3.9 collective-permute-done
  120.2 7.4 all_gather.26
  128.2 1.3 collective-permute-start
  129.5 4.3 collective-permute-done
  134.8 6.6 all_gather.26
  142.0 1.3 collective-permute-start
  143.4 4.3 collective-permute-done
  148.6 6.6 all_gather.26
  155.9 1.3 collective-permute-start
  157.2 5.0 collective-permute-done
  163.1 6.4 all_gather.26
  170.1 1.3 collective-permute-start
  171.4 5.8 collective-permute-done
  178.2 6.4 all_gather.26
  185.2 1.3 collective-permute-start
  186.5 5.8 collective-permute-done
  193.2 6.4 all_gather.26
  200.2 1.3 collective-permute-start
  201.5 5.8 collective-permute-done
  208.2 6.4 all_gather.26
  215.2 1.3 collective-permute-start
  216.5 5.8 collective-permute-done
  223.2 6.4 all_gather.26
  230.2 1.3 collective-permute-start
  231.5 5.8 collective-permute-done
  238.2 6.4 all_gather.26
  245.2 1.3 collective-permute-start
  246.5 5.8 collective-permute-done
  253.3 6.4 all_gather.26
  260.2 1.3 collective-permute-start
  261.6 8.0 collective-permute-done
  270.6 6.4 all_gather.26
  278.9 8.2 collective-permute-done
  288.0 6.4 all_gather.26
  296.3 8.2 collective-permute-done
  305.4 6.4 all_gather.26
  313.7 8.2 collective-permute-done
  322.8 6.4 all_gather.26
  331.1 8.2 collective-permute-done
  340.2 6.4 all_gather.26
  348.5 61.6 %collective-permute-done = bf16[32,1024]{1,0:T(8,128)(2,1)S(1)} collective-permute-done((bf16[32,1024]{1,0:T(8,128)(2,1)}, bf16[32,1024]{1,0:T(8,128)(2,1)S(1)}, u32[]{:S(2)}, u32[]{:S(2)}) %collective-permute-start) | collective-permute-done | bytes 65568 | tf_op jit(solution)/shard_map/while/body/eval_jaxpr/ppermute | solution.py:13
  411.1 6.4 all_gather.26
  417.4 6.6 conditional.2
  417.4 6.6 fusion
  425.3 8.2 collective-permute-done
  434.5 6.4 all_gather.26
  440.8 6.6 conditional.2
  440.8 6.6 fusion
  448.7 8.2 collective-permute-done
  457.9 6.4 all_gather.26
  464.3 6.6 conditional.2
  464.3 6.6 fusion
  472.2 8.2 collective-permute-done
  481.3 6.4 all_gather.26
  487.7 6.6 conditional.2
  487.7 6.6 fusion
  494.6 10.8 all-reduce
  505.7 18.6 %all-gather.2 = f32[8,4,1024]{2,1,0:T(4,128)S(1)} all-gather(f32[1,4,1024]{2,1,0:T(4,128)S(1)} %broadcast_in_dim_reshape.3), channel_id=1, replica_groups=mesh['section'=16,'dp'=8,'mp'=4] {'dp'}, dimensions={0}, use_global_device_ids=true | all-gather | bytes 147456 | tf_op jit(solution)/shard_map/all_gather | solution.py:108
  528.6 823.8 %all-gather.8.cloned.1.call-done = f32[4096,8,2,4]{1,3,2,0:T(4,128)} async-done(((f32[8,8,2,4]{1,3,2,0:T(4,128)}), f32[4096,8,2,4]{1,3,2,0:T(4,128)}) %all-gather.8.cloned.1.call-update) | async-done | bytes 1048592 | tf_op jit(solution)/shard_map/all_gather | solution.py:115
  1352.4 9.9 reduce_sum.9
  (106 shorter events, 55.3 us)
Async XLA Ops:
  7.2 16.9 %copy-start = (bf16[1,128,1024]{2,1,0:T(8,128)(2,1)S(1)}, bf16[1,128,1024]{2,1,0:T(8,128)(2,1)}, u32[]{:S(2)}) copy-start(bf16[1,128,1024]{2,1,0:T(8,128)(2,1)} %param.13) | copy-start | bytes 786436
  7.2 106.0 %all-gather.6.cloned.1.call-start = ((), (), s32[]{:S(2)}) async-start(), calls=%async_computation | async-start | bytes 9437184 | tf_op jit(solution)/shard_map/all_gather | solution.py:46
  7.9 1344.5 %all-gather.8.cloned.1.call-start = ((), (), s32[]{:S(2)}) async-start(), calls=%async_computation.1 | async-start | bytes 16809984 | tf_op jit(solution)/shard_map/all_gather | solution.py:115
  113.8 380.4 %copy-start.2 = (bf16[1,1024,64]{1,2,0:T(8,128)(2,1)S(1)}, bf16[1,1024,64]{1,2,0:T(8,128)(2,1)}, u32[]{:S(2)}) copy-start(bf16[1,1024,64]{1,2,0:T(8,128)(2,1)} %param.17) | copy-start | bytes 393220
  113.8 410.4 %copy-start.1 = (f32[1,2,1024]{2,1,0:T(2,128)S(1)}, f32[1,2,1024]{2,1,0:T(2,128)}, u32[]{:S(2)}) copy-start(f32[1,2,1024]{2,1,0:T(2,128)} %param.18) | copy-start | bytes 24580
  113.9 5.4 collective-permute-start
  128.2 5.6 collective-permute-start
  142.0 5.6 collective-permute-start
  155.9 6.3 collective-permute-start
  170.1 7.1 collective-permute-start
  185.2 7.1 collective-permute-start
  200.2 7.1 collective-permute-start
  215.2 7.1 collective-permute-start
  230.2 7.1 collective-permute-start
  245.2 7.1 collective-permute-start
  260.2 9.4 collective-permute-start
  277.5 9.5 collective-permute-start
  295.0 9.5 collective-permute-start
  312.4 9.5 collective-permute-start
  329.8 9.5 collective-permute-start
  347.2 62.9 %collective-permute-start = (bf16[32,1024]{1,0:T(8,128)(2,1)}, bf16[32,1024]{1,0:T(8,128)(2,1)S(1)}, u32[]{:S(2)}, u32[]{:S(2)}) collective-permute-start(bf16[32,1024]{1,0:T(8,128)(2,1)} %get-tuple-element.299), channel_id=1, source_target_pairs={{32,0},{64,32},{96,64},{128,96},{160,128},{192,160},{224,192},{256... | collective-permute-start | bytes 196616 | tf_op jit(solution)/shard_map/while/body/eval_jaxpr/ppermute | solution.py:13
  424.0 9.5 collective-permute-start
  447.4 9.5 collective-permute-start
  470.9 9.5 collective-permute-start
  505.7 856.6 %copy-start.3 = (f32[1,4,1024]{2,1,0:T(4,128)}, f32[1,4,1024]{2,1,0:T(4,128)S(1)}, u32[]{:S(2)}) copy-start(f32[1,4,1024]{2,1,0:T(4,128)S(1)} %broadcast_in_dim_reshape.3) | copy-start | bytes 49156
Sparse Core Ops, SparseCore 0:
  10.1 103.0 all-gather.5
  528.7 823.6 all-gather.7
